TPU v7x, 32 devices: a whole 2x2x4 slice. The times are simulated.
32 devices in a mesh: dp: 8 (over z, core), shard: 4 (over y, x).
Axes of the slice: x: 2, y: 2, z: 4, core: 2. Of those that a mesh axis runs over, the one named last changes fastest.
Arguments:
- text_in: bfloat16 [32, 512, 768], P(('dp', 'shard')), may hold values from -6 to 6
- layout_in: bfloat16 [32, 512, 192], P(('dp', 'shard')), may hold values from -6 to 6
- lengths: int32 [32], P(('dp', 'shard')), may hold values from 40 to 512, as said below
- text_attn: bfloat16 [768, 3072], P(('dp', 'shard')), may hold values from -2 to 2
- text_w1: bfloat16 [768, 3072], P(('dp', 'shard')), may hold values from -0.21875 to 0.21875
- text_w2: bfloat16 [3072, 768], P(('dp', 'shard')), may hold values from -0.109375 to 0.109375
- text_vectors: bfloat16 [9216], P(('dp', 'shard')), may hold values from -2 to 2
- layout_attn: bfloat16 [768, 192], P(('dp', 'shard')), may hold values from -2 to 2
- layout_w1: bfloat16 [192, 768], P(None, ('dp', 'shard')), may hold values from -0.4375 to 0.4375
- layout_w2: bfloat16 [768, 192], P(('dp', 'shard')), may hold values from -0.21875 to 0.21875
- layout_vectors: bfloat16 [2304], P(('dp', 'shard')), may hold values from -2 to 2
- cot_text: bfloat16 [32, 512, 768], P(('dp', 'shard')), may hold values from -6 to 6
- cot_layout: bfloat16 [32, 512, 192], P(('dp', 'shard')), may hold values from -6 to 6
Outputs:
- out_text: bfloat16 [32, 512, 768], P(('dp', 'shard'))
- out_layout: bfloat16 [32, 512, 192], P(('dp', 'shard'))
- grad_text_in: float32 [32, 512, 768], P(('dp', 'shard'))
- grad_layout_in: float32 [32, 512, 192], P(('dp', 'shard'))
- grad_text_attn: float32 [768, 3072], P(('dp', 'shard'))
- grad_text_w1: float32 [768, 3072], P(('dp', 'shard'))
- grad_text_w2: float32 [3072, 768], P(('dp', 'shard'))
- grad_text_vectors: float32 [9216], P(('dp', 'shard'))
- grad_layout_attn: float32 [768, 192], P(('dp', 'shard'))
- grad_layout_w1: float32 [192, 768], P(None, ('dp', 'shard'))
- grad_layout_w2: float32 [768, 192], P(('dp', 'shard'))
- grad_layout_vectors: float32 [2304], P(('dp', 'shard'))
Inputs may be any that keep to these rules, and one draw needn't show every extreme that they name: `lengths`: the real tokens of a page fill its first slots; the first page of the batch is full and the second holds 40 tokens.
All inputs are finite; a program needn't handle non-finite values.
Results may differ from a plain program's by a relative error of at most 0.012.
The roundings to bfloat16 on the way count: a program that leaves them out, or rounds other values in their place, can miss the bound.
Values may be sent and summed in bfloat16 or wider, within the bound.
No kernel may reach another device: no remote copies, remote signals or barrier semaphores. Data moves between devices by JAX's collectives and lax.ppermute only.
A program may use at most 192 MiB of HBM per device.

v0:
```python
import functools

import jax
import jax.numpy as jnp
from jax import lax
from jax.experimental import pallas as pl
from jax.experimental.pallas import tpu as pltpu
from jax.sharding import PartitionSpec as P


H = 12
HD = 64
LHD = 16


EPS = 1e-05
NEG = -1000000000.0


def normalize(values, scale_row, shift_row):
    centered = values - jnp.mean(values, -1, keepdims=True)
    variance = jnp.mean(centered * centered, -1, keepdims=True)
    return centered * lax.rsqrt(variance + EPS) * scale_row + shift_row


def gelu_exact(values):
    return 0.5 * values * (1.0 + lax.erf(values * (0.5 ** 0.5)))


def vector_parts(packed, width):
    pieces = [packed[index * width : (index + 1) * width] for index in range(8)]
    return pieces + [packed[8 * width :]]


def block_of(attn, index, width, columns):
    if columns:
        return attn[:, index * width : (index + 1) * width]
    return attn[index * width : (index + 1) * width]


def project_three(inputs, attn, packed, width, columns):
    if columns:
        three = attn[:, 0 : 3 * width].reshape(width, 3, width)
        mixed = jnp.einsum("sd,dje->sje", inputs, three, preferred_element_type=jnp.float32)
    else:
        three = attn[0 : 3 * width].reshape(3, width, width)
        mixed = jnp.einsum("sd,jde->sje", inputs, three, preferred_element_type=jnp.float32)
    pieces = vector_parts(packed.astype(jnp.float32), width)
    offsets = jnp.stack([pieces[0], jnp.zeros_like(pieces[0]), pieces[1]])
    return (mixed + offsets[None]).astype(jnp.bfloat16)


def attend(text_three, layout_three, length):
    return attn_fwd_heads(
        jnp.reshape(length, (1,)).astype(jnp.int32),
        text_three.transpose(1, 2, 0),
        layout_three.transpose(1, 2, 0),
        (HD ** (-0.5), LHD ** (-0.5)),
    )


def _nn(a, b):
    return lax.dot_general(a, b, (((1,), (0,)), ((), ())), preferred_element_type=jnp.float32)


def _nt(a, b):
    return lax.dot_general(a, b, (((1,), (1,)), ((), ())), preferred_element_type=jnp.float32)


def attn_back_kernel(len_ref, text_ref, dc_ref, layout_ref, dcl_ref, lse_ref, text_out, layout_out, *, scales):
    text_scale, layout_scale = scales
    query, key, value = text_ref[0], text_ref[1], text_ref[2]
    query_l, key_l, value_l = layout_ref[0], layout_ref[1], layout_ref[2]
    scores = _nn(key.T, query) * text_scale + _nn(key_l.T, query_l) * layout_scale
    keys = lax.broadcasted_iota(jnp.int32, scores.shape, 0)
    scores = jnp.where(keys < len_ref[0], scores, NEG)
    probs = jnp.exp(scores - lse_ref[0])
    text_dp = _nn(value.T, dc_ref[...])
    layout_dp = _nn(value_l.T, dcl_ref[...])
    text_ds = probs * (text_dp - jnp.sum(probs * text_dp, 0, keepdims=True))
    layout_ds = probs * (layout_dp - jnp.sum(probs * layout_dp, 0, keepdims=True))
    text_g = text_ds.astype(jnp.bfloat16)
    joint_g = (text_ds + layout_ds).astype(jnp.bfloat16)
    weights = probs.astype(jnp.bfloat16)
    text_out[0] = (_nn(key, text_g) * text_scale).astype(text_out.dtype)
    text_out[1] = (_nt(query, text_g) * text_scale).astype(text_out.dtype)
    text_out[2] = _nt(dc_ref[...], weights).astype(text_out.dtype)
    layout_out[0] = (_nn(key_l, joint_g) * layout_scale).astype(layout_out.dtype)
    layout_out[1] = (_nt(query_l, joint_g) * layout_scale).astype(layout_out.dtype)
    layout_out[2] = _nt(dcl_ref[...], weights).astype(layout_out.dtype)


def attn_back_heads(length, text_t, dc_t, layout_t, dcl_t, lse, scales):
    parts, width, slots = text_t.shape
    narrow = layout_t.shape[1]
    wide, thin = width // H, narrow // H
    text_spec = pl.BlockSpec((parts, wide, slots), lambda h, n: (0, h, 0))
    layout_spec = pl.BlockSpec((parts, thin, slots), lambda h, n: (0, h, 0))
    flops = H * slots * slots * 2 * (4 * wide + 4 * thin)
    return pl.pallas_call(
        functools.partial(attn_back_kernel, scales=scales),
        grid_spec=pltpu.PrefetchScalarGridSpec(
            num_scalar_prefetch=1,
            grid=(H,),
            in_specs=[
                text_spec,
                pl.BlockSpec((wide, slots), lambda h, n: (h, 0)),
                layout_spec,
                pl.BlockSpec((thin, slots), lambda h, n: (h, 0)),
                pl.BlockSpec((1, 1, slots), lambda h, n: (h, 0, 0)),
            ],
            out_specs=[text_spec, layout_spec],
        ),
        out_shape=[
            jax.ShapeDtypeStruct(text_t.shape, jnp.bfloat16),
            jax.ShapeDtypeStruct(layout_t.shape, jnp.bfloat16),
        ],
        compiler_params=pltpu.CompilerParams(dimension_semantics=("arbitrary",)),
        cost_estimate=pl.CostEstimate(
            flops=flops,
            transcendentals=H * slots * slots,
            bytes_accessed=slots * (8 * width + 8 * narrow + 4 * H),
        ),
    )(length, text_t, dc_t, layout_t, dcl_t, lse)


def attn_fwd_kernel(len_ref, text_ref, layout_ref, ctx_out, ctxl_out, lse_out, *, scales):
    text_scale, layout_scale = scales
    query, key, value = text_ref[0], text_ref[1], text_ref[2]
    query_l, key_l, value_l = layout_ref[0], layout_ref[1], layout_ref[2]
    scores = _nn(key.T, query) * text_scale + _nn(key_l.T, query_l) * layout_scale
    keys = lax.broadcasted_iota(jnp.int32, scores.shape, 0)
    scores = jnp.where(keys < len_ref[0], scores, NEG)
    top = jnp.max(scores, 0, keepdims=True)
    exponent = jnp.exp(scores - top)
    total = jnp.sum(exponent, 0, keepdims=True)
    weights = (exponent / total).astype(jnp.bfloat16)
    ctx_out[...] = _nn(value, weights).astype(ctx_out.dtype)
    ctxl_out[...] = _nn(value_l, weights).astype(ctxl_out.dtype)
    lse_out[0] = top + jnp.log(total)


def attn_fwd_heads(length, text_t, layout_t, scales):
    parts, width, slots = text_t.shape
    narrow = layout_t.shape[1]
    wide, thin = width // H, narrow // H
    flops = H * slots * slots * 2 * (2 * wide + 2 * thin)
    return pl.pallas_call(
        functools.partial(attn_fwd_kernel, scales=scales),
        grid_spec=pltpu.PrefetchScalarGridSpec(
            num_scalar_prefetch=1,
            grid=(H,),
            in_specs=[
                pl.BlockSpec((parts, wide, slots), lambda h, n: (0, h, 0)),
                pl.BlockSpec((parts, thin, slots), lambda h, n: (0, h, 0)),
            ],
            out_specs=[
                pl.BlockSpec((wide, slots), lambda h, n: (h, 0)),
                pl.BlockSpec((thin, slots), lambda h, n: (h, 0)),
                pl.BlockSpec((1, 1, slots), lambda h, n: (h, 0, 0)),
            ],
        ),
        out_shape=[
            jax.ShapeDtypeStruct((width, slots), jnp.bfloat16),
            jax.ShapeDtypeStruct((narrow, slots), jnp.bfloat16),
            jax.ShapeDtypeStruct((H, 1, slots), jnp.float32),
        ],
        compiler_params=pltpu.CompilerParams(dimension_semantics=("arbitrary",)),
        cost_estimate=pl.CostEstimate(
            flops=flops,
            transcendentals=H * slots * slots,
            bytes_accessed=slots * (8 * width + 8 * narrow + 4 * H),
        ),
    )(length, text_t, layout_t)


def attend_back(text_three, layout_three, length, log_total, text_grad, layout_grad):
    return attn_back_heads(
        jnp.reshape(length, (1,)).astype(jnp.int32),
        text_three.transpose(1, 2, 0),
        text_grad.T,
        layout_three.transpose(1, 2, 0),
        layout_grad.T,
        log_total,
        (HD ** (-0.5), LHD ** (-0.5)),
    )


def project_back(attn, width, columns, grad_t, first_grad):
    if columns:
        three = attn[:, 0 : 3 * width].reshape(width, 3, width)
        input_grad = first_grad + jnp.einsum(
            "jes,dje->sd", grad_t, three, preferred_element_type=jnp.float32
        )
    else:
        three = attn[0 : 3 * width].reshape(3, width, width)
        input_grad = first_grad + jnp.einsum(
            "jes,jde->sd", grad_t, three, preferred_element_type=jnp.float32
        )
    column_sums = jnp.sum(grad_t.astype(jnp.float32), 2)
    return (input_grad, grad_t, column_sums[0], column_sums[2])


def branch_forward(inputs, context, attn, packed, first, second, width, columns):
    pieces = vector_parts(packed.astype(jnp.float32), width)
    out_block = block_of(attn, 3, width, columns)
    first_res = inputs.astype(jnp.float32) + (
        jnp.dot(context, out_block, preferred_element_type=jnp.float32) + pieces[2]
    )
    hidden = normalize(first_res, pieces[3], pieces[4])
    inner = (
        jnp.dot(hidden.astype(jnp.bfloat16), first, preferred_element_type=jnp.float32) + pieces[8]
    )
    activated = gelu_exact(inner).astype(jnp.bfloat16)
    second_res = hidden + (
        jnp.dot(activated, second, preferred_element_type=jnp.float32) + pieces[5]
    )
    result = normalize(second_res, pieces[6], pieces[7])
    return (result, (first_res, inner, second_res))


def branch_backward(attn, packed, first, second, width, columns, kept_rows, grad_out):
    first_res, inner, second_res = kept_rows
    pieces = vector_parts(packed.astype(jnp.float32), width)
    hidden, first_pull = jax.vjp(normalize, first_res, pieces[3], pieces[4])
    _, second_pull = jax.vjp(normalize, second_res, pieces[6], pieces[7])
    grad_second, late_scale, late_shift = second_pull(grad_out)
    round_second = grad_second.astype(jnp.bfloat16)
    activated, gelu_pull = jax.vjp(gelu_exact, inner)
    (grad_inner,) = gelu_pull(jnp.dot(round_second, second.T, preferred_element_type=jnp.float32))
    round_inner = grad_inner.astype(jnp.bfloat16)
    grad_hidden = grad_second + jnp.dot(round_inner, first.T, preferred_element_type=jnp.float32)
    grad_first, early_scale, early_shift = first_pull(grad_hidden)
    round_first = grad_first.astype(jnp.bfloat16)
    out_block = block_of(attn, 3, width, columns)
    grad_ctx = jnp.dot(round_first, out_block.T, preferred_element_type=jnp.float32).astype(
        jnp.bfloat16
    )
    operands = (
        hidden.astype(jnp.bfloat16),
        activated.astype(jnp.bfloat16),
        round_first,
        round_second,
        round_inner,
    )
    vector_sums = (
        jnp.sum(grad_first, 0),
        early_scale,
        early_shift,
        jnp.sum(grad_second, 0),
        late_scale,
        late_shift,
        jnp.sum(grad_inner, 0),
    )
    return (grad_first, grad_ctx, operands, vector_sums)


def branch_back_a(packed, second, width, kept_rows, grad_out):
    first_res, inner, second_res = kept_rows
    pieces = vector_parts(packed.astype(jnp.float32), width)
    hidden = normalize(first_res, pieces[3], pieces[4])
    _, second_pull = jax.vjp(normalize, second_res, pieces[6], pieces[7])
    grad_second, late_scale, late_shift = second_pull(grad_out)
    round_second = grad_second.astype(jnp.bfloat16)
    activated, gelu_pull = jax.vjp(gelu_exact, inner)
    (grad_inner,) = gelu_pull(jnp.dot(round_second, second.T, preferred_element_type=jnp.float32))
    round_inner = grad_inner.astype(jnp.bfloat16)
    return (
        grad_second,
        round_second,
        grad_inner,
        round_inner,
        hidden.astype(jnp.bfloat16),
        activated.astype(jnp.bfloat16),
        late_scale,
        late_shift,
    )


def branch_back_b(attn, packed, first, width, columns, kept_rows, part_a):
    first_res, _, _ = kept_rows
    grad_second, round_second, grad_inner, round_inner, hidden_low, active_low, late_scale, late_shift = part_a
    pieces = vector_parts(packed.astype(jnp.float32), width)
    _, first_pull = jax.vjp(normalize, first_res, pieces[3], pieces[4])
    grad_hidden = grad_second + jnp.dot(round_inner, first.T, preferred_element_type=jnp.float32)
    grad_first, early_scale, early_shift = first_pull(grad_hidden)
    round_first = grad_first.astype(jnp.bfloat16)
    out_block = block_of(attn, 3, width, columns)
    grad_ctx = jnp.dot(round_first, out_block.T, preferred_element_type=jnp.float32).astype(
        jnp.bfloat16
    )
    operands = (hidden_low, active_low, round_first, round_second, round_inner)
    vector_sums = (
        jnp.sum(grad_first, 0),
        early_scale,
        early_shift,
        jnp.sum(grad_second, 0),
        late_scale,
        late_shift,
        jnp.sum(grad_inner, 0),
    )
    return (grad_first, grad_ctx, operands, vector_sums)


def page_forward(text_rows, layout_rows, length, weights):
    (text_attn, text_first, text_second, text_packed, layout_attn, _, _, layout_packed) = weights
    width = text_rows.shape[1]
    narrow = layout_rows.shape[1]
    valid = jnp.arange(text_rows.shape[0], dtype=jnp.int32) < length
    text_three = project_three(text_rows, text_attn, text_packed, width, True)
    layout_three = project_three(layout_rows, layout_attn, layout_packed, narrow, False)
    text_ctx, layout_ctx, log_total = attend(text_three, layout_three, length)
    text_out, text_kept = branch_forward(
        text_rows, text_ctx.T, text_attn, text_packed, text_first, text_second, width, True
    )
    mask = valid[:, None].astype(jnp.float32)
    kept_page = (text_three, layout_three, text_ctx, layout_ctx, log_total, text_kept)
    return ((text_out * mask).astype(jnp.bfloat16), kept_page)


def page_back_ffn(length, kept_page, text_cot, weights):
    text_attn, _, text_second, text_packed = weights[:4]
    text_kept = kept_page[5]
    width = text_attn.shape[0]
    slots = text_cot.shape[0]
    valid = jnp.arange(slots, dtype=jnp.int32) < length
    mask = valid[:, None].astype(jnp.float32)
    return branch_back_a(
        text_packed, text_second, width, text_kept, text_cot.astype(jnp.float32) * mask
    )


def page_back_attn(text_rows, layout_rows, length, kept_page, text_a, layout_cot, weights):
    (
        text_attn,
        text_first,
        _,
        text_packed,
        layout_attn,
        layout_first,
        layout_second,
        layout_packed,
    ) = weights
    text_three, layout_three, _, layout_ctx, log_total, text_kept = kept_page
    width = text_rows.shape[1]
    narrow = layout_rows.shape[1]
    slots = text_rows.shape[0]
    valid = jnp.arange(slots, dtype=jnp.int32) < length
    mask = valid[:, None].astype(jnp.float32)
    layout_out, layout_kept = branch_forward(
        layout_rows,
        layout_ctx.T,
        layout_attn,
        layout_packed,
        layout_first,
        layout_second,
        narrow,
        False,
    )
    layout_back = branch_backward(
        layout_attn,
        layout_packed,
        layout_first,
        layout_second,
        narrow,
        False,
        layout_kept,
        layout_cot.astype(jnp.float32) * mask,
    )
    text_back = branch_back_b(text_attn, text_packed, text_first, width, True, text_kept, text_a)
    text_res_grad, text_ctx_grad, text_ops, text_sums = text_back
    layout_res_grad, layout_ctx_grad, layout_ops, layout_sums = layout_back
    text_three_grad, layout_three_grad = attend_back(
        text_three, layout_three, length, log_total, text_ctx_grad, layout_ctx_grad
    )
    text_in_grad, text_rounded, text_query_bias, text_value_bias = project_back(
        text_attn, width, True, text_three_grad, text_res_grad
    )
    layout_in_grad, layout_rounded, layout_query_bias, layout_value_bias = project_back(
        layout_attn, narrow, False, layout_three_grad, layout_res_grad
    )
    hidden_low, active_low, first_low, second_low, inner_low = layout_ops
    three_w = jnp.einsum(
        "sd,jes->jde", layout_rows, layout_rounded, preferred_element_type=jnp.float32
    ).reshape(3 * narrow, narrow)
    out_w = jnp.einsum("ds,se->de", layout_ctx, first_low, preferred_element_type=jnp.float32)
    layout_attn_grad = jnp.concatenate([three_w, out_w], 0)
    layout_first_grad = jnp.einsum(
        "sd,sf->df", hidden_low, inner_low, preferred_element_type=jnp.float32
    )
    layout_second_grad = jnp.einsum(
        "sf,sd->fd", active_low, second_low, preferred_element_type=jnp.float32
    )
    layout_vec_grad = jnp.concatenate([layout_query_bias, layout_value_bias] + list(layout_sums))
    text_vec_grad = jnp.concatenate([text_query_bias, text_value_bias] + list(text_sums))
    small_terms = (
        text_vec_grad,
        layout_attn_grad,
        layout_first_grad,
        layout_second_grad,
        layout_vec_grad,
    )
    layout_low = (layout_out * mask).astype(jnp.bfloat16)
    grads = (text_in_grad, layout_in_grad)
    return (layout_low, grads, small_terms, text_rounded, text_ops[2])


def flat_rows(values):
    return values.reshape(-1, values.shape[-1])


AXES = ("dp", "shard")


def rows_for(size, width, aligned):
    rows = -(-size // width)
    if aligned:
        rows = -(-rows // 8) * 8
    return rows


def pack_rows(pieces, width, aligned):
    flat = jnp.concatenate([piece.reshape(-1) for piece in pieces])
    rows = rows_for(flat.shape[0], width, aligned)
    return jnp.pad(flat, (0, rows * width - flat.shape[0])).reshape(rows, width)


def unpack_small(flat, count, shapes):
    sizes = [rows * cols for rows, cols in shapes]
    offsets = [sum(sizes[:index]) for index in range(len(sizes))]
    parts = [flat[:, offset : offset + size] for offset, size in zip(offsets, sizes)]
    (attn_rows, attn_cols), (w1_rows, w1_cols), (w2_rows, w2_cols) = shapes[1:4]
    return (
        parts[0].reshape(-1),
        parts[1].reshape(count * attn_rows, attn_cols),
        parts[2].reshape(count, w1_rows, w1_cols).transpose(1, 0, 2).reshape(w1_rows, count * w1_cols),
        parts[3].reshape(count * w2_rows, w2_cols),
        parts[4].reshape(-1),
    )


def gather_weights(text_attn, text_w1, text_w2, text_vectors, layout_attn, layout_w1, layout_w2, layout_vectors):
    rows, width = text_attn.shape
    aligned = rows % 8 == 0
    small = (text_vectors, layout_attn, layout_w1, layout_w2, layout_vectors)
    small_rows = pack_rows(small, width, aligned)
    first = jnp.concatenate([text_attn, text_w1, small_rows], 0)
    first_all = lax.all_gather(first, AXES, axis=0, tiled=True)
    count = first_all.shape[0] // first.shape[0]
    first_all = first_all.reshape(count, first.shape[0], width)
    full_attn = first_all[:, :rows].reshape(count * rows, width)
    full_w1 = first_all[:, rows : 2 * rows].reshape(count * rows, width)
    small_flat = first_all[:, 2 * rows :].reshape(count, -1)
    shapes = [(1, text_vectors.shape[0]), layout_attn.shape, layout_w1.shape, layout_w2.shape, (1, layout_vectors.shape[0])]
    full_small = unpack_small(small_flat, count, shapes)
    full_w2 = lax.all_gather(text_w2, AXES, axis=0, tiled=True)
    return (full_attn, full_w1, full_w2) + full_small


def small_blocks(count, text_vec_grad, layout_attn_grad, layout_w1_grad, layout_w2_grad, layout_vec_grad):
    local_w1_cols = layout_w1_grad.shape[1] // count
    return (
        text_vec_grad.reshape(count, -1),
        layout_attn_grad.reshape(count, -1),
        layout_w1_grad.reshape(layout_w1_grad.shape[0], count, local_w1_cols)
        .transpose(1, 0, 2)
        .reshape(count, -1),
        layout_w2_grad.reshape(count, -1),
        layout_vec_grad.reshape(count, -1),
    )


def scatter_late(count, grad_attn, small_grads):
    width = grad_attn.shape[1]
    rows = grad_attn.shape[0] // count
    blocks = small_blocks(count, *small_grads)
    joined = jnp.concatenate(blocks, 1)
    size = joined.shape[1]
    small_rows = rows_for(size, width, rows % 8 == 0)
    joined = jnp.pad(joined, ((0, 0), (0, small_rows * width - size))).reshape(count, small_rows, width)
    packed = jnp.concatenate([grad_attn.reshape(count, rows, width), joined], 1)
    summed = lax.psum_scatter(
        packed.reshape(-1, width).astype(jnp.bfloat16), AXES, scatter_dimension=0, tiled=True
    ).astype(jnp.float32)
    attn_part = summed[:rows]
    flat = summed[rows:].reshape(-1)
    sizes = [block.shape[1] for block in blocks]
    offsets = [sum(sizes[:index]) for index in range(len(sizes))]
    parts = [flat[offset : offset + size] for offset, size in zip(offsets, sizes)]
    _, layout_attn_grad, layout_w1_grad, layout_w2_grad, _ = small_grads
    local_w1_cols = layout_w1_grad.shape[1] // count
    return (
        attn_part,
        parts[0],
        parts[1].reshape(layout_attn_grad.shape[0] // count, layout_attn_grad.shape[1]),
        parts[2].reshape(layout_w1_grad.shape[0], local_w1_cols),
        parts[3].reshape(layout_w2_grad.shape[0] // count, layout_w2_grad.shape[1]),
        parts[4],
    )


def pack_early(count, grad_first, grad_second):
    width = grad_first.shape[1]
    rows = grad_first.shape[0] // count
    packed = jnp.concatenate(
        [grad_first.reshape(count, rows, width), grad_second.reshape(count, rows, width)], 1
    )
    return packed.reshape(-1, width).astype(jnp.bfloat16)


def scatter_early(count, packed, second_shape):
    rows = packed.shape[0] // (2 * count)
    summed = lax.psum_scatter(packed, AXES, scatter_dimension=0, tiled=True).astype(jnp.float32)
    return (summed[:rows], summed[rows:].reshape(-1, second_shape[1]))


def body(
    text_in,
    layout_in,
    lengths,
    text_attn,
    text_w1,
    text_w2,
    text_vectors,
    layout_attn,
    layout_w1,
    layout_w2,
    layout_vectors,
    cot_text,
    cot_layout,
):
    count = lax.psum(1, AXES)
    weights = gather_weights(
        text_attn, text_w1, text_w2, text_vectors, layout_attn, layout_w1, layout_w2, layout_vectors
    )

    page_weights = (None,) * len(weights)
    out_text, kept_all = jax.vmap(page_forward, in_axes=(0, 0, 0, page_weights))(
        text_in, layout_in, lengths, weights
    )
    text_a = jax.vmap(page_back_ffn, in_axes=(0, 0, 0, page_weights))(
        lengths, kept_all, cot_text, weights
    )
    round_second, round_inner, text_hidden, text_active = text_a[1], text_a[3], text_a[4], text_a[5]
    early = (
        jnp.einsum("sd,sf->df", flat_rows(text_hidden), flat_rows(round_inner), preferred_element_type=jnp.float32),
        jnp.einsum("sf,sd->fd", flat_rows(text_active), flat_rows(round_second), preferred_element_type=jnp.float32),
    )
    packed = pack_early(count, *early)
    packed, text_a, kept_all = lax.optimization_barrier((packed, text_a, kept_all))
    grad_first, grad_second = scatter_early(count, packed, early[1].shape)
    out_layout, (text_grad, layout_grad), small_terms, text_rounded, text_first_low = jax.vmap(
        page_back_attn, in_axes=(0, 0, 0, 0, 0, 0, page_weights)
    )(text_in, layout_in, lengths, kept_all, text_a, cot_layout, weights)
    totals = tuple(jnp.sum(term, 0) for term in small_terms)
    three_part = jnp.einsum(
        "psd,pjes->dje", text_in, text_rounded, preferred_element_type=jnp.float32
    ).reshape(text_in.shape[2], -1)
    out_part = jnp.einsum(
        "pds,pse->de", kept_all[2], text_first_low, preferred_element_type=jnp.float32
    )
    summed = scatter_late(count, jnp.concatenate([three_part, out_part], 1), totals)
    return (
        out_text,
        out_layout,
        text_grad,
        layout_grad,
        summed[0],
        grad_first,
        grad_second,
        summed[1],
        summed[2],
        summed[3],
        summed[4],
        summed[5],
    )


def solution(mesh):
    placed = (
        P(("dp", "shard"), None, None),
        P(("dp", "shard"), None, None),
        P(("dp", "shard")),
        P(("dp", "shard"), None),
        P(("dp", "shard"), None),
        P(("dp", "shard"), None),
        P(("dp", "shard")),
        P(("dp", "shard"), None),
        P(None, ("dp", "shard")),
        P(("dp", "shard"), None),
        P(("dp", "shard")),
        P(("dp", "shard"), None, None),
        P(("dp", "shard"), None, None),
    )
    return jax.shard_map(
        body,
        mesh=mesh,
        in_specs=placed,
        out_specs=(
            P(("dp", "shard"), None, None),
            P(("dp", "shard"), None, None),
            P(("dp", "shard"), None, None),
            P(("dp", "shard"), None, None),
            P(("dp", "shard"), None),
            P(("dp", "shard"), None),
            P(("dp", "shard"), None),
            P(("dp", "shard")),
            P(("dp", "shard"), None),
            P(None, ("dp", "shard")),
            P(("dp", "shard"), None),
            P(("dp", "shard")),
        ),
        check_vma=False,
    )
```

profile of v0, /device:TPU:0, one launch (start us, length us, event | category | flops | bytes accessed | tf_op | source)
XLA Modules:
  0.0 579.7 jit_solution(284045546087248520)
XLA Ops:
  9.8 1.4 concatenate.34
  11.3 1.7 pad_maximum_fusion.4
  15.7 88.5 %all-gather.3.cloned.1.call-done = bf16[1792,3072]{1,0:T(8,128)(2,1)} async-done(((bf16[56,3072]{1,0:T(8,128)(2,1)}), bf16[1792,3072]{1,0:T(8,128)(2,1)}) %all-gather.3.cloned.1.call-update) | async-done | bytes 11010064 | tf_op jit(solution)/shard_map/all_gather | solution.py:448
  104.2 1.5 slice.197
  106.6 1.0 slice.201
  110.8 6.9 %fusion.66 = (bf16[32,24,3072]{2,1,0:T(8,128)(2,1)S(1)}, bf16[32,24,3072]{2,1,0:T(8,128)(2,1)}) fusion(bf16[32,56,3072]{2,1,0:T(8,128)(2,1)} %bitcast.222), kind=kLoop, calls=%fused_computation.155 | loop fusion | bytes 18874368 | tf_op jit(solution)/shard_map/slice | solution.py:451
  117.6 2.1 copy-done.1
  119.7 2.0 slice.196
  121.7 5.0 copy.35
  126.8 2.2 reshape.640
  130.4 1.3 slice.219
  131.7 1.6 fusion.72
  134.8 2.2 fusion.9.layout_ref
  137.0 4.6 add_convert_fusion.text_ref
  141.6 13.4 %vmap__.2 = (bf16[768,512]{1,0:T(8,128)(2,1)}, bf16[192,512]{1,0:T(8,128)(2,1)}, f32[12,1,512]{2,1,0:T(1,128)}) custom-call(s32[1]{0:T(128)} %copy.66.len_ref, bf16[3,768,512]{2,1,0:T(8,128)(2,1)} %add_convert_fusion.text_ref, bf16[3,192,512]{2,1,0:T(8,128)(2,1)} %fusion.9.layout_ref), custom_call_target="tpu_custom_call" | custom-call | flops 1006632960 | bytes 3956736 | tf_op jit(solution)/shard_map/vmap()/pallas_call | solution.py:148
  155.0 2.7 fusion.73
  158.6 1.2 fusion.100
  159.9 8.2 %multiply_convert_fusion = (bf16[512,3072]{1,0:T(8,128)(2,1)}, f32[512,3072]{1,0:T(8,128)}) fusion(f32[3072]{0:T(1024)S(1)} %copy-done.41, bf16[768,3072]{1,0:T(8,128)(2,1)} %bitcast.228, bf16[1,512,768]{2,1,0:T(8,128)(2,1)S(1)} %fusion.15), kind=kOutput, calls=%fused_computation.3 | convolution fusion | flops 2425356288 | bytes 14954496 | tf_op jit(solution)/shard_map/vmap()/dot_general | solution.py:212
  168.1 2.0 fusion.68
  170.1 6.0 %fusion.74 = (f32[512]{0:T(512)S(1)}, f32[1,512,768]{2,1,0:T(8,128)S(1)}) fusion(f32[768]{0:T(1024)S(1)} %copy-done.52, bf16[512,3072]{1,0:T(8,128)(2,1)} %get-tuple-element.112, bf16[3072,768]{1,0:T(8,128)(2,1)} %all-gather.5.cloned.1.call-done, f32[768]{0:T(1024)S(1)} %copy-done.31, f32[768]{0:T(1024)S(1)} %copy-done.29, f32[512]{0:T(512)S(1)} %add_rsqrt_fusion, ...), kind=kOutput, calls=%fused_computation.163 | convolution fusion | flops 2418671104 | bytes 11025408 | tf_op jit(solution)/shard_map/vmap()/dot_general | solution.py:216
  178.1 1.7 fusion.65
  180.9 1.6 copy-done.65
  182.5 4.6 convolution_convert_fusion.1
  187.1 8.5 %reshape.646 = bf16[32,24,3072]{2,1,0:T(8,128)(2,1)} reshape(bf16[3072,768]{1,0:T(8,128)(2,1)} %convolution_convert_fusion.1) | data formatting | bytes 9437184 | tf_op jit(solution)/shard_map/reshape | solution.py:506
  195.6 2.3 copy.37
  197.9 7.5 %multiply_add_fusion = f32[512,3072]{1,0:T(8,128)S(1)} fusion(f32[512,3072]{1,0:T(8,128)} %get-tuple-element.113, f32[3072]{0:T(1024)S(1)} %copy-done.41, bf16[3072,768]{1,0:T(8,128)(2,1)} %all-gather.5.cloned.1.call-done, bf16[1,512,768]{2,1,0:T(8,128)(2,1)} %copy-done.22), kind=kOutput, calls=%fused_computation.2 | convolution fusion | flops 2436366336 | bytes 18100224 | tf_op jit(solution)/shard_map/vmap()/dot_general | solution.py:266
  205.4 2.1 convert_bitcast_fusion
  207.5 1.8 copy-done
  209.3 2.8 convolution_convert_fusion.2
  213.4 3.9 pad_maximum_fusion
  217.7 6.9 %multiply_reduce_fusion = (bf16[768]{0:T(1024)(128)(2,1)}, f32[512]{0:T(512)S(1)}, bf16[768]{0:T(1024)(128)(2,1)}, f32[1,512,768]{2,1,0:T(8,128)S(1)}) fusion(f32[1,512,768]{2,1,0:T(8,128)S(1)} %get-tuple-element.35, f32[512]{0:T(512)S(1)} %fusion.56, f32[512]{0:T(512)S(1)} %broadcast_multiply_fusion.2, f32[768]{0:T(1024)S(1)} %copy-done.29, ...), kind=kOutput, calls=%fused_computation.20 | convolution fusion | flops 2419456000 | bytes 12595200 | tf_op jit(solution)/shard_map/vmap()/dot_general | solution.py:285
  225.3 3.6 fusion.10.dc_ref
  231.1 2.5 reshape.649
  234.4 1.1 slice.171
  235.5 1.3 fusion.75
  237.0 1.1 reshape.651
  238.1 1.4 multiply_convert_fusion.1
  241.2 0.9 fusion.62
  242.1 1.1 multiply_add_fusion.1
  243.3 1.1 multiply_reduce_fusion.8
  246.4 1.6 fusion.67
  248.0 1.0 convolution_convert_fusion.7
  249.0 24.1 %vmap__.3 = (bf16[3,768,512]{2,1,0:T(8,128)(2,1)}, bf16[3,192,512]{2,1,0:T(8,128)(2,1)}) custom-call(s32[1]{0:T(128)} %copy.66.len_ref, bf16[3,768,512]{2,1,0:T(8,128)(2,1)} %add_convert_fusion.text_ref, bf16[768,512]{1,0:T(8,128)(2,1)} %fusion.10.dc_ref, bf16[3,192,512]{2,1,0:T(8,128)(2,1)} %fusion.9.layout_ref, bf16[192,512]{1,0:T(8,128)(2,1)} %fusion.19.dcl_ref, ...), custom_call_target="tpu_custom_call" | custom-call | flops 2013265920 | bytes 3956736 | tf_op jit(solution)/shard_map/vmap()/pallas_call | solution.py:100
  273.1 2.1 convolution_convert_fusion.6
  275.2 1.8 reduce.38
  278.4 2.1 reduce.37
  280.6 3.2 reduce_sum.408
  284.9 1.0 reshape.661
  285.9 1.2 copy.44
  287.1 1.6 fusion.13
  289.7 3.0 reshape.662
  292.7 1.2 copy.47
  294.6 1.1 concatenate.41
  297.0 0.9 convolution_convert_fusion.3
  298.8 2.0 fusion
  300.8 2.5 pad_maximum_fusion.2
  303.3 6.6 %copy.42 = bf16[768,3072]{1,0:T(8,128)(2,1)} copy(bf16[768,3072]{0,1:T(8,128)(2,1)} %pad_maximum_fusion.2) | data formatting | bytes 9437184 | tf_op jit(solution)/shard_map/concatenate | solution.py:562
  310.0 5.7 pad_maximum_fusion.1
  316.2 2.6 fusion.14
  318.9 5.0 bitcast_add_fusion
  323.9 105.3 %reduce-scatter.3.cloned.1.call-done = bf16[32,3072]{1,0:T(8,128)(2,1)} async-done(((bf16[1024,3072]{1,0:T(8,128)(2,1)}), bf16[32,3072]{1,0:T(8,128)(2,1)}) %reduce-scatter.3.cloned.1.call-update) | async-done | bytes 196624 | tf_op jit(solution)/shard_map/reduce_scatter | solution.py:482
  429.2 1.0 convert_element_type.181
  435.5 134.7 %reduce-scatter.5.cloned.1.call-done = bf16[48,3072]{1,0:T(8,128)(2,1)} async-done(((bf16[1536,3072]{1,0:T(8,128)(2,1)}), bf16[48,3072]{1,0:T(8,128)(2,1)}) %reduce-scatter.5.cloned.1.call-update) | async-done | bytes 294928 | tf_op jit(solution)/shard_map/reduce_scatter | solution.py:513
  570.2 1.7 fusion.69
  (244 shorter events, 37.2 us)
Async XLA Ops:
  7.2 97.0 %all-gather.3.cloned.1.call-start = ((), (), s32[]{:S(2)}) async-start(), calls=%async_computation.2 | async-start | bytes 11354112 | tf_op jit(solution)/shard_map/all_gather | solution.py:448
  13.0 157.1 %all-gather.5.cloned.1.call-start = ((), (), s32[]{:S(2)}) async-start(), calls=%async_computation.3 | async-start | bytes 4866048 | tf_op jit(solution)/shard_map/all_gather | solution.py:456
  13.8 415.4 %reduce-scatter.3.cloned.1.call-start = ((), (), s32[]{:S(2)}) async-start(), calls=%async_computation.4 | async-start | bytes 6488064 | tf_op jit(solution)/shard_map/reduce_scatter | solution.py:482
  106.5 1.7 copy-start.10
  117.6 2.1 copy-start.1
  126.8 14.8 %copy-start.2 = (bf16[768,2304]{0,1:T(8,128)(2,1)}, bf16[768,2304]{0,1:T(8,128)(2,1)S(1)}, u32[]{:S(2)}) copy-start(bf16[768,2304]{0,1:T(8,128)(2,1)S(1)} %copy.35) | copy-start | bytes 10616836
  133.3 106.2 %copy-start.33 = (f32[192]{0:T(256)}, f32[192]{0:T(256)S(1)}, u32[]{:S(2)}) copy-start(f32[192]{0:T(256)S(1)} %get-tuple-element.104) | copy-start | bytes 2308
  141.6 13.4 %copy-start.53 = (f32[768]{0:T(1024)S(1)}, f32[768]{0:T(1024)}, u32[]{:S(2)}) copy-start(f32[768]{0:T(1024)} %get-tuple-element.97) | copy-start | bytes 9220
  158.6 1.2 copy-start.41
  159.9 10.2 %copy-start.52 = (f32[768]{0:T(1024)S(1)}, f32[768]{0:T(1024)}, u32[]{:S(2)}) copy-start(f32[768]{0:T(1024)} %get-tuple-element.94) | copy-start | bytes 9220
  176.1 1.1 copy-start.14
  176.1 1.1 copy-start.30
  176.1 1.1 copy-start.32
  176.5 1.6 copy-start.40
  179.8 2.7 copy-start.65
  180.0 37.7 %copy-start.8 = (f32[1,512,768]{2,1,0:T(8,128)}, f32[1,512,768]{2,1,0:T(8,128)S(1)}, u32[]{:S(2)}) copy-start(f32[1,512,768]{2,1,0:T(8,128)S(1)} %get-tuple-element.33) | copy-start | bytes 4718596
  205.4 4.0 copy-start
  205.4 3.9 copy-start.23
  207.5 5.8 %slice-start = ((s8[4718592]{0:T(1024)(128)(4,1)}), s8[4194304]{0:T(1024)(128)(4,1)S(1)}, s32[]{:S(2)}) async-start(s8[4718592]{0:T(1024)(128)(4,1)} %bitcast.214), calls=%async_computation.6 | async-start | bytes 8388608
  209.3 4.0 slice-start.1
  225.3 71.4 %copy-start.4 = (f32[1,512,768]{2,1,0:T(8,128)}, f32[1,512,768]{2,1,0:T(8,128)S(1)}, u32[]{:S(2)}) copy-start(f32[1,512,768]{2,1,0:T(8,128)S(1)} %get-tuple-element.75) | copy-start | bytes 4718596
  225.3 3.6 copy-start.36
  228.9 1.4 copy-start.9
  231.1 4.5 copy-start.54
  234.3 5.1 copy-start.11
  234.4 2.6 copy-start.19
  235.5 3.9 copy-start.20
  238.1 1.5 copy-start.16
  238.1 1.5 copy-start.44
  238.1 1.5 copy-start.50
  239.5 1.7 copy-start.51
  242.1 1.1 copy-start.12
  242.1 1.2 copy-start.34
  243.3 1.2 copy-start.39
  243.3 1.3 copy-start.21
  244.6 32.4 %copy-start.6 = (f32[1,512,192]{1,2,0:T(8,128)}, f32[1,512,192]{1,2,0:T(8,128)S(1)}, u32[]{:S(2)}) copy-start(f32[1,512,192]{1,2,0:T(8,128)S(1)} %get-tuple-element.71) | copy-start | bytes 1179652
  249.0 24.1 %copy-start.26 = (bf16[1,512,192]{1,2,0:T(8,128)(2,1)S(1)}, bf16[1,512,192]{1,2,0:T(8,128)(2,1)}, u32[]{:S(2)}) copy-start(bf16[1,512,192]{1,2,0:T(8,128)(2,1)} %param.14) | copy-start | bytes 589828
  280.5 3.2 copy-start.47
  280.5 3.3 copy-start.56
  280.5 3.3 copy-start.55
  280.5 3.3 copy-start.46
  280.5 3.3 copy-start.42
  280.5 3.3 copy-start.43
  280.5 4.2 copy-start.27
  280.5 4.3 copy-start.18
  283.7 2.2 copy-start.13
  284.8 2.3 copy-start.35
  289.6 4.6 copy-start.48
  289.6 4.6 copy-start.60
  289.6 4.6 copy-start.62
  289.6 4.6 copy-start.61
  289.6 4.6 copy-start.59
  289.7 4.6 copy-start.58
  289.7 4.6 copy-start.57
  289.7 4.6 copy-start.49
  289.7 4.9 copy-start.28
  292.7 2.0 copy-start.17
  295.8 1.1 copy-start.64
  297.0 1.7 copy-start.7
  297.0 1.8 copy-start.63
  315.7 254.6 %reduce-scatter.5.cloned.1.call-start = ((), (), s32[]{:S(2)}) async-start(), calls=%async_computation.5 | async-start | bytes 9732096 | tf_op jit(solution)/shard_map/reduce_scatter | solution.py:513
  315.7 3.2 copy-start.3
  316.2 2.7 copy-start.5
  429.2 5.6 copy-start.15
  (8 other events, 7.2 us)
Sparse Core Ops, SparseCore 0:
  13.2 90.9 all-gather.2
  107.1 62.1 all-gather.4
  315.8 113.3 reduce-scatter.2
  435.0 135.1 reduce-scatter.4
where the time goes:
time: 584 us; the launch traced here: 580 us
  waiting for transfers between devices  330 us (57%)
  local copies, waits for them, and re-layouts  85.3 us (15%)
  matrix products  71.6 us (12%)
  other arithmetic  39.5 us (7%)
  Pallas kernels  37.4 us (6%)
  between operations  16 us (3%)
    reduce_scatter x1, waiting for transfers between devices, scatter_early(): lax.psum_scatter(packed, AXES, scatter_dimension=0, tiled=True)  135 us
    reduce_scatter x1, waiting for transfers between devices, scatter_late(): lax.psum_scatter(packed.reshape(-1, width).astype(jnp.bfloat16), AXES, sc...  105 us
    all_gather x1, waiting for transfers between devices, gather_weights(): first_all = lax.all_gather(first, AXES, axis=0, tiled=True)  88.5 us
    pallas_call x1, Pallas kernels, attn_back_heads(): pl.pallas_call(functools.partial(attn_back_kernel, scales=scales), grid_s...  24.1 us
    pallas_call x1, Pallas kernels, attn_fwd_heads(): pl.pallas_call(functools.partial(attn_fwd_kernel, scales=scales), grid_sp...  13.4 us
    unnamed x150, local copies, waits for them, and re-layouts  13.3 us
  transfers between devices with their start and end apart: 4, of which 3 were waited for; matrix products, arithmetic and copies ran while one was open for 11% of the time, Pallas kernels for 2%

commit v1 on v0

--- a/solution.py
+++ b/solution.py
@@ -255,31 +255,29 @@
     return (grad_first, grad_ctx, operands, vector_sums)
 
 
-def branch_back_a(packed, second, width, kept_rows, grad_out):
+def branch_back_a(packed, width, kept_rows, grad_out):
     first_res, inner, second_res = kept_rows
     pieces = vector_parts(packed.astype(jnp.float32), width)
     hidden = normalize(first_res, pieces[3], pieces[4])
     _, second_pull = jax.vjp(normalize, second_res, pieces[6], pieces[7])
     grad_second, late_scale, late_shift = second_pull(grad_out)
     round_second = grad_second.astype(jnp.bfloat16)
-    activated, gelu_pull = jax.vjp(gelu_exact, inner)
-    (grad_inner,) = gelu_pull(jnp.dot(round_second, second.T, preferred_element_type=jnp.float32))
-    round_inner = grad_inner.astype(jnp.bfloat16)
     return (
         grad_second,
         round_second,
-        grad_inner,
-        round_inner,
         hidden.astype(jnp.bfloat16),
-        activated.astype(jnp.bfloat16),
+        gelu_exact(inner).astype(jnp.bfloat16),
         late_scale,
         late_shift,
     )
 
 
-def branch_back_b(attn, packed, first, width, columns, kept_rows, part_a):
-    first_res, _, _ = kept_rows
-    grad_second, round_second, grad_inner, round_inner, hidden_low, active_low, late_scale, late_shift = part_a
+def branch_back_b(attn, packed, first, second, width, columns, kept_rows, part_a):
+    first_res, inner, _ = kept_rows
+    grad_second, round_second, hidden_low, active_low, late_scale, late_shift = part_a
+    _, gelu_pull = jax.vjp(gelu_exact, inner)
+    (grad_inner,) = gelu_pull(jnp.dot(round_second, second.T, preferred_element_type=jnp.float32))
+    round_inner = grad_inner.astype(jnp.bfloat16)
     pieces = vector_parts(packed.astype(jnp.float32), width)
     _, first_pull = jax.vjp(normalize, first_res, pieces[3], pieces[4])
     grad_hidden = grad_second + jnp.dot(round_inner, first.T, preferred_element_type=jnp.float32)
@@ -319,22 +317,20 @@
 
 
 def page_back_ffn(length, kept_page, text_cot, weights):
-    text_attn, _, text_second, text_packed = weights[:4]
+    text_attn, _, _, text_packed = weights[:4]
     text_kept = kept_page[5]
     width = text_attn.shape[0]
     slots = text_cot.shape[0]
     valid = jnp.arange(slots, dtype=jnp.int32) < length
     mask = valid[:, None].astype(jnp.float32)
-    return branch_back_a(
-        text_packed, text_second, width, text_kept, text_cot.astype(jnp.float32) * mask
-    )
+    return branch_back_a(text_packed, width, text_kept, text_cot.astype(jnp.float32) * mask)
 
 
 def page_back_attn(text_rows, layout_rows, length, kept_page, text_a, layout_cot, weights):
     (
         text_attn,
         text_first,
-        _,
+        text_second,
         text_packed,
         layout_attn,
         layout_first,
@@ -367,7 +363,9 @@
         layout_kept,
         layout_cot.astype(jnp.float32) * mask,
     )
-    text_back = branch_back_b(text_attn, text_packed, text_first, width, True, text_kept, text_a)
+    text_back = branch_back_b(
+        text_attn, text_packed, text_first, text_second, width, True, text_kept, text_a
+    )
     text_res_grad, text_ctx_grad, text_ops, text_sums = text_back
     layout_res_grad, layout_ctx_grad, layout_ops, layout_sums = layout_back
     text_three_grad, layout_three_grad = attend_back(
@@ -402,7 +400,7 @@
     )
     layout_low = (layout_out * mask).astype(jnp.bfloat16)
     grads = (text_in_grad, layout_in_grad)
-    return (layout_low, grads, small_terms, text_rounded, text_ops[2])
+    return (layout_low, grads, small_terms, text_rounded, text_ops[2], text_ops[4])
 
 
 def flat_rows(values):
@@ -470,7 +468,7 @@
     )
 
 
-def scatter_late(count, grad_attn, small_grads):
+def scatter_late(count, grad_attn, grad_first, small_grads):
     width = grad_attn.shape[1]
     rows = grad_attn.shape[0] // count
     blocks = small_blocks(count, *small_grads)
@@ -478,12 +476,15 @@
     size = joined.shape[1]
     small_rows = rows_for(size, width, rows % 8 == 0)
     joined = jnp.pad(joined, ((0, 0), (0, small_rows * width - size))).reshape(count, small_rows, width)
-    packed = jnp.concatenate([grad_attn.reshape(count, rows, width), joined], 1)
+    packed = jnp.concatenate(
+        [grad_attn.reshape(count, rows, width), grad_first.reshape(count, rows, width), joined], 1
+    )
     summed = lax.psum_scatter(
         packed.reshape(-1, width).astype(jnp.bfloat16), AXES, scatter_dimension=0, tiled=True
     ).astype(jnp.float32)
     attn_part = summed[:rows]
-    flat = summed[rows:].reshape(-1)
+    first_part = summed[rows : 2 * rows]
+    flat = summed[2 * rows :].reshape(-1)
     sizes = [block.shape[1] for block in blocks]
     offsets = [sum(sizes[:index]) for index in range(len(sizes))]
     parts = [flat[offset : offset + size] for offset, size in zip(offsets, sizes)]
@@ -491,27 +492,13 @@
     local_w1_cols = layout_w1_grad.shape[1] // count
     return (
         attn_part,
+        first_part,
         parts[0],
         parts[1].reshape(layout_attn_grad.shape[0] // count, layout_attn_grad.shape[1]),
         parts[2].reshape(layout_w1_grad.shape[0], local_w1_cols),
         parts[3].reshape(layout_w2_grad.shape[0] // count, layout_w2_grad.shape[1]),
         parts[4],
     )
-
-
-def pack_early(count, grad_first, grad_second):
-    width = grad_first.shape[1]
-    rows = grad_first.shape[0] // count
-    packed = jnp.concatenate(
-        [grad_first.reshape(count, rows, width), grad_second.reshape(count, rows, width)], 1
-    )
-    return packed.reshape(-1, width).astype(jnp.bfloat16)
-
-
-def scatter_early(count, packed, second_shape):
-    rows = packed.shape[0] // (2 * count)
-    summed = lax.psum_scatter(packed, AXES, scatter_dimension=0, tiled=True).astype(jnp.float32)
-    return (summed[:rows], summed[rows:].reshape(-1, second_shape[1]))
 
 
 def body(
@@ -541,38 +528,43 @@
     text_a = jax.vmap(page_back_ffn, in_axes=(0, 0, 0, page_weights))(
         lengths, kept_all, cot_text, weights
     )
-    round_second, round_inner, text_hidden, text_active = text_a[1], text_a[3], text_a[4], text_a[5]
-    early = (
-        jnp.einsum("sd,sf->df", flat_rows(text_hidden), flat_rows(round_inner), preferred_element_type=jnp.float32),
-        jnp.einsum("sf,sd->fd", flat_rows(text_active), flat_rows(round_second), preferred_element_type=jnp.float32),
-    )
-    packed = pack_early(count, *early)
-    packed, text_a, kept_all = lax.optimization_barrier((packed, text_a, kept_all))
-    grad_first, grad_second = scatter_early(count, packed, early[1].shape)
-    out_layout, (text_grad, layout_grad), small_terms, text_rounded, text_first_low = jax.vmap(
-        page_back_attn, in_axes=(0, 0, 0, 0, 0, 0, page_weights)
-    )(text_in, layout_in, lengths, kept_all, text_a, cot_layout, weights)
+    round_second, text_hidden, text_active = text_a[1], text_a[2], text_a[3]
+    second_grad = jnp.einsum(
+        "sf,sd->fd", flat_rows(text_active), flat_rows(round_second), preferred_element_type=jnp.float32
+    ).astype(jnp.bfloat16)
+    second_grad, text_a, kept_all = lax.optimization_barrier((second_grad, text_a, kept_all))
+    grad_second = lax.psum_scatter(second_grad, AXES, scatter_dimension=0, tiled=True).astype(
+        jnp.float32
+    )
+    out_layout, (text_grad, layout_grad), small_terms, text_rounded, text_first_low, round_inner = (
+        jax.vmap(page_back_attn, in_axes=(0, 0, 0, 0, 0, 0, page_weights))(
+            text_in, layout_in, lengths, kept_all, text_a, cot_layout, weights
+        )
+    )
     totals = tuple(jnp.sum(term, 0) for term in small_terms)
+    first_grad = jnp.einsum(
+        "sd,sf->df", flat_rows(text_hidden), flat_rows(round_inner), preferred_element_type=jnp.float32
+    )
     three_part = jnp.einsum(
         "psd,pjes->dje", text_in, text_rounded, preferred_element_type=jnp.float32
     ).reshape(text_in.shape[2], -1)
     out_part = jnp.einsum(
         "pds,pse->de", kept_all[2], text_first_low, preferred_element_type=jnp.float32
     )
-    summed = scatter_late(count, jnp.concatenate([three_part, out_part], 1), totals)
+    summed = scatter_late(count, jnp.concatenate([three_part, out_part], 1), first_grad, totals)
     return (
         out_text,
         out_layout,
         text_grad,
         layout_grad,
         summed[0],
-        grad_first,
+        summed[1],
         grad_second,
-        summed[1],
         summed[2],
         summed[3],
         summed[4],
         summed[5],
+        summed[6],
     )
 
 

time: 584 us -> 497 us (0.85)
  waiting for transfers between devices: 330 us -> 246 us
    reduce_scatter x1, waiting for transfers between devices: 135 us -> 6.01 us  [body(): lax.psum_scatter(second_grad, AXES, scatter_dimension=0, tiled=True)]
    reduce_scatter x1, waiting for transfers between devices: 105 us -> 147 us  [scatter_late(): lax.psum_scatter(packed.reshape(-1, width).astype(jnp.bfloat16), AXES, sc...]
    reshape x2 -> x0, local copies, waits for them, and re-layouts: 9.27 us -> none  [the longest x1 8.48 us: pack_early(): grad_second.reshape(count, rows, width)]
    unnamed x150 -> x136, local copies, waits for them, and re-layouts: 13.3 us -> 12.6 us
  transfers between devices with their start and end apart: 4 -> 4, of which waited for: 3 -> 4; matrix products, arithmetic and copies ran while one was open for 11% -> 25% of each run, Pallas kernels for 2% -> 8%
where the time goes in v1:
time: 497 us; the launch traced here: 492 us
  waiting for transfers between devices  246 us (49%)
  local copies, waits for them, and re-layouts  86 us (17%)
  matrix products  71.9 us (14%)
  Pallas kernels  37.4 us (8%)
  other arithmetic  35.3 us (7%)
  between operations  15.6 us (3%)
    reduce_scatter x1, waiting for transfers between devices, scatter_late(): lax.psum_scatter(packed.reshape(-1, width).astype(jnp.bfloat16), AXES, sc...  147 us
    all_gather x1, waiting for transfers between devices, gather_weights(): first_all = lax.all_gather(first, AXES, axis=0, tiled=True)  89.1 us
    pallas_call x1, Pallas kernels, attn_back_heads(): pl.pallas_call(functools.partial(attn_back_kernel, scales=scales), grid_s...  24.1 us
    pallas_call x1, Pallas kernels, attn_fwd_heads(): pl.pallas_call(functools.partial(attn_fwd_kernel, scales=scales), grid_sp...  13.4 us
    unnamed x136, local copies, waits for them, and re-layouts  12.6 us
  transfers between devices with their start and end apart: 4, of which 4 were waited for; matrix products, arithmetic and copies ran while one was open for 25% of the time, Pallas kernels for 8%

profile of v1, /device:TPU:0, one launch (start us, length us, event | category | flops | bytes accessed | tf_op | source)
XLA Modules:
  0.0 492.2 jit_solution(15464518239319422762)
XLA Ops:
  9.8 1.4 concatenate.30
  11.3 1.7 pad_maximum_fusion.3
  15.1 89.1 %all-gather.3.cloned.1.call-done = bf16[1792,3072]{1,0:T(8,128)(2,1)} async-done(((bf16[56,3072]{1,0:T(8,128)(2,1)}), bf16[1792,3072]{1,0:T(8,128)(2,1)}) %all-gather.3.cloned.1.call-update) | async-done | bytes 11010064 | tf_op jit(solution)/shard_map/all_gather | solution.py:446
  104.2 1.5 slice.193
  111.3 6.9 %fusion.69 = (bf16[32,24,3072]{2,1,0:T(8,128)(2,1)S(1)}, bf16[32,24,3072]{2,1,0:T(8,128)(2,1)}) fusion(bf16[32,56,3072]{2,1,0:T(8,128)(2,1)} %bitcast.234), kind=kLoop, calls=%fused_computation.159 | loop fusion | bytes 18874368 | tf_op jit(solution)/shard_map/slice | solution.py:449
  118.2 2.2 copy-done
  120.4 2.1 slice.192
  122.5 5.0 %copy.35 = bf16[768,2304]{0,1:T(8,128)(2,1)S(1)} copy(bf16[768,2304]{1,0:T(8,128)(2,1)} %slice.192) | data formatting | bytes 7077888 | tf_op jit(solution)/shard_map/vmap()/slice | solution.py:43
  127.6 1.7 slice.215
  129.3 1.6 fusion.75
  132.4 2.2 fusion.15.layout_ref
  134.5 4.7 add_convert_fusion.text_ref
  139.2 13.4 %vmap__.2 = (bf16[768,512]{1,0:T(8,128)(2,1)}, bf16[192,512]{1,0:T(8,128)(2,1)}, f32[12,1,512]{2,1,0:T(1,128)}) custom-call(s32[1]{0:T(128)} %copy.66.len_ref, bf16[3,768,512]{2,1,0:T(8,128)(2,1)} %add_convert_fusion.text_ref, bf16[3,192,512]{2,1,0:T(8,128)(2,1)} %fusion.15.layout_ref), custom_call_target="tpu_custom_call" | custom-call | flops 1006632960 | bytes 3956736 | tf_op jit(solution)/shard_map/vmap()/pallas_call | solution.py:148
  152.6 2.7 fusion.76
  156.3 8.1 %add_bitcast_fusion = (f32[1,512,3072]{2,1,0:T(8,128)}, bf16[512,3072]{1,0:T(8,128)(2,1)}) fusion(f32[3072]{0:T(1024)S(1)} %slice-done.2, bf16[768,3072]{1,0:T(8,128)(2,1)} %bitcast.240, bf16[1,512,768]{2,1,0:T(8,128)(2,1)S(1)} %fusion.21), kind=kOutput, calls=%fused_computation.9 | convolution fusion | flops 2425356288 | bytes 14954496 | tf_op jit(solution)/shard_map/vmap()/dot_general | solution.py:212
  164.4 2.1 fusion.71
  166.5 2.8 all-gather.5.cloned.1.call-done
  169.3 6.0 %fusion.77 = (f32[512]{0:T(512)S(1)}, f32[1,512,768]{2,1,0:T(8,128)S(1)}) fusion(f32[768]{0:T(1024)S(1)} %copy-done.51, bf16[512,3072]{1,0:T(8,128)(2,1)} %get-tuple-element.83, bf16[3072,768]{1,0:T(8,128)(2,1)} %all-gather.5.cloned.1.call-done, f32[768]{0:T(1024)S(1)} %get-tuple-element.97, f32[768]{0:T(1024)S(1)} %get-tuple-element.98, ...), kind=kOutput, calls=%fused_computation.167 | convolution fusion | flops 2418671104 | bytes 11025408 | tf_op jit(solution)/shard_map/vmap()/dot_general | solution.py:216
  177.3 1.7 fusion.68
  180.1 1.6 copy-done.56
  181.8 4.4 convolution_convert_fusion.2
  188.7 8.1 %fusion.80 = (bf16[3072]{0:T(1024)(128)(2,1)}, bf16[1,512,3072]{2,1,0:T(8,128)(2,1)S(1)}) fusion(f32[1,512,3072]{2,1,0:T(8,128)} %get-tuple-element.34, bf16[3072,768]{1,0:T(8,128)(2,1)} %all-gather.5.cloned.1.call-done, bf16[1,512,768]{2,1,0:T(8,128)(2,1)S(1)} %copy-done.22), kind=kOutput, calls=%fused_computation.170 | convolution fusion | flops 2437936128 | bytes 14948352 | tf_op jit(solution)/shard_map/vmap()/dot_general | solution.py:279
  196.8 7.1 %multiply_reduce_fusion = (bf16[768]{0:T(1024)(128)(2,1)}, f32[512]{0:T(512)S(1)}, bf16[768]{0:T(1024)(128)(2,1)}, f32[1,512,768]{2,1,0:T(8,128)S(1)}) fusion(f32[1,512,768]{2,1,0:T(8,128)S(1)} %get-tuple-element.36, f32[512]{0:T(512)S(1)} %fusion.59, f32[512]{0:T(512)S(1)} %broadcast_multiply_fusion.2, f32[768]{0:T(1024)S(1)} %get-tuple-element.98, ...), kind=kOutput, calls=%fused_computation.25 | convolution fusion | flops 2419456000 | bytes 12595200 | tf_op jit(solution)/shard_map/vmap()/dot_general | solution.py:283
  206.0 1.3 fusion.78
  208.0 4.2 reshape.629
  212.3 2.4 copy.37
  214.7 2.1 reshape.631
  216.8 1.7 multiply_convert_fusion.1
  221.4 1.1 multiply_add_fusion
  222.6 1.2 multiply_reduce_fusion.8
  224.8 1.9 fusion.25.dcl_ref
  226.7 3.1 fusion.16.dc_ref
  229.8 24.1 %vmap__.3 = (bf16[3,768,512]{2,1,0:T(8,128)(2,1)}, bf16[3,192,512]{2,1,0:T(8,128)(2,1)}) custom-call(s32[1]{0:T(128)} %copy.66.len_ref, bf16[3,768,512]{2,1,0:T(8,128)(2,1)} %add_convert_fusion.text_ref, bf16[768,512]{1,0:T(8,128)(2,1)} %fusion.16.dc_ref, bf16[3,192,512]{2,1,0:T(8,128)(2,1)} %fusion.15.layout_ref, bf16[192,512]{1,0:T(8,128)(2,1)} %fusion.25.dcl_ref, ...), custom_call_target="tpu_custom_call" | custom-call | flops 2013265920 | bytes 3956736 | tf_op jit(solution)/shard_map/vmap()/pallas_call | solution.py:100
  253.9 2.2 reduce_sum.406
  256.0 2.7 reduce.37
  258.8 2.2 convolution_convert_fusion.3
  261.0 2.0 fusion.5
  263.0 2.5 pad_maximum_fusion.1
  265.5 6.6 %copy.41 = bf16[768,3072]{1,0:T(8,128)(2,1)} copy(bf16[768,3072]{0,1:T(8,128)(2,1)} %pad_maximum_fusion.1) | data formatting | bytes 9437184 | tf_op jit(solution)/shard_map/concatenate | solution.py:554
  272.1 1.9 fusion.106
  274.0 2.4 copy.42
  277.7 1.8 reduce.38
  279.6 2.9 fusion.70
  283.1 1.2 reduce_sum.421
  284.3 1.3 reduce_sum.426
  285.6 1.2 reduce_sum.433
  286.8 1.3 reduce_sum.435
  288.6 1.4 concatenate.35
  290.0 1.3 reduce.40
  291.4 1.4 reshape.645
  293.8 1.2 copy.47
  296.0 1.2 copy.44
  297.2 1.6 fusion.19
  298.8 1.6 copy.46
  300.5 3.4 reshape.643
  305.7 1.1 concatenate.36
  309.0 2.8 convolution_convert_fusion
  311.8 5.1 %pad_maximum_fusion = bf16[32,56,3072]{2,1,0:T(8,128)(2,1)} fusion(bf16[32,8,3072]{2,1,0:T(8,128)(2,1)S(1)} %bitcast.239, bf16[32,24,3072]{2,1,0:T(8,128)(2,1)S(1)} %convolution_convert_fusion, bf16[32,24,3072]{2,1,0:T(8,128)(2,1)S(1)} %bitcast.227), kind=kLoop, calls=%fused_computation | loop fusion | flops 33030144 | bytes 22020096 | tf_op jit(solution)/shard_map/concatenate | solution.py:479
  317.0 2.5 fusion.20
  320.0 4.9 bitcast_add_fusion
  324.9 6.0 %reduce-scatter.5.cloned.1.call-done = bf16[96,768]{1,0:T(8,128)(2,1)} async-done(((bf16[3072,768]{1,0:T(8,128)(2,1)}), bf16[96,768]{1,0:T(8,128)(2,1)}) %reduce-scatter.5.cloned.1.call-update) | async-done | bytes 147472 | tf_op jit(solution)/shard_map/reduce_scatter | solution.py:536
  330.9 1.6 convert_element_type.177
  332.5 147.1 %reduce-scatter.3.cloned.1.call-done = bf16[56,3072]{1,0:T(8,128)(2,1)} async-done(((bf16[1792,3072]{1,0:T(8,128)(2,1)}), bf16[56,3072]{1,0:T(8,128)(2,1)}) %reduce-scatter.3.cloned.1.call-update) | async-done | bytes 344080 | tf_op jit(solution)/shard_map/reduce_scatter | solution.py:482
  479.7 1.1 convert_element_type.176
  (226 shorter events, 37.4 us)
Async XLA Ops:
  7.2 97.0 %all-gather.3.cloned.1.call-start = ((), (), s32[]{:S(2)}) async-start(), calls=%async_computation.2 | async-start | bytes 11354112 | tf_op jit(solution)/shard_map/all_gather | solution.py:446
  13.0 156.3 %all-gather.5.cloned.1.call-start = ((), (), s32[]{:S(2)}) async-start(), calls=%async_computation.3 | async-start | bytes 4866048 | tf_op jit(solution)/shard_map/all_gather | solution.py:454
  13.8 317.1 %reduce-scatter.5.cloned.1.call-start = ((), (), s32[]{:S(2)}) async-start(), calls=%async_computation.5 | async-start | bytes 4866048 | tf_op jit(solution)/shard_map/reduce_scatter | solution.py:536
  106.5 11.6 %copy-start.14 = (bf16[4,8,8,3072]{3,1,2,0:T(8,128)(2,1)}, bf16[4,8,8,3072]{3,1,2,0:T(8,128)(2,1)S(1)}, u32[]{:S(2)}) copy-start(bf16[4,8,8,3072]{3,1,2,0:T(8,128)(2,1)S(1)} %copy.53) | copy-start | bytes 4718596
  109.5 8.7 %copy-start.28 = (f32[9216]{0:T(1024)}, f32[9216]{0:T(1024)S(1)}, u32[]{:S(2)}) copy-start(f32[9216]{0:T(1024)S(1)} %reshape.650) | copy-start | bytes 110596
  110.1 59.2 %copy-start.29 = (f32[768]{0:T(1024)}, f32[768]{0:T(1024)S(1)}, u32[]{:S(2)}) copy-start(f32[768]{0:T(1024)S(1)} %get-tuple-element.97) | copy-start | bytes 9220
  118.2 2.2 copy-start
  127.6 11.6 %copy-start.1 = (bf16[768,2304]{0,1:T(8,128)(2,1)}, bf16[768,2304]{0,1:T(8,128)(2,1)S(1)}, u32[]{:S(2)}) copy-start(bf16[768,2304]{0,1:T(8,128)(2,1)S(1)} %copy.35) | copy-start | bytes 10616836
  155.3 14.0 %copy-start.30 = (f32[512]{0:T(512)}, f32[512]{0:T(512)S(1)}, u32[]{:S(2)}) copy-start(f32[512]{0:T(512)S(1)} %broadcast_multiply_fusion.4) | copy-start | bytes 6148
  155.6 0.7 slice-start.2
  155.6 13.7 %copy-start.38 = (f32[512]{0:T(512)}, f32[512]{0:T(512)S(1)}, u32[]{:S(2)}) copy-start(f32[512]{0:T(512)S(1)} %add_rsqrt_fusion) | copy-start | bytes 6148
  156.3 13.0 %copy-start.51 = (f32[768]{0:T(1024)S(1)}, f32[768]{0:T(1024)}, u32[]{:S(2)}) copy-start(f32[768]{0:T(1024)} %get-tuple-element.96) | copy-start | bytes 9220
  175.4 1.1 copy-start.17
  175.7 1.6 copy-start.41
  179.0 2.7 copy-start.56
  179.3 0.9 copy-start.21
  179.3 17.5 %copy-start.9 = (f32[1,512,768]{2,1,0:T(8,128)}, f32[1,512,768]{2,1,0:T(8,128)S(1)}, u32[]{:S(2)}) copy-start(f32[1,512,768]{2,1,0:T(8,128)S(1)} %get-tuple-element.33) | copy-start | bytes 4718596
  187.5 1.1 copy-start.22
  196.8 7.1 %copy-start.57 = (bf16[1,512,3072]{2,1,0:T(8,128)(2,1)}, bf16[1,512,3072]{2,1,0:T(8,128)(2,1)S(1)}, u32[]{:S(2)}) copy-start(bf16[1,512,3072]{2,1,0:T(8,128)(2,1)S(1)} %get-tuple-element.125) | copy-start | bytes 9437188
  204.0 1.3 copy-start.27
  204.0 2.0 copy-start.52
  204.6 100.5 %copy-start.3 = (f32[1,512,768]{2,1,0:T(8,128)}, f32[1,512,768]{2,1,0:T(8,128)S(1)}, u32[]{:S(2)}) copy-start(f32[1,512,768]{2,1,0:T(8,128)S(1)} %get-tuple-element.75) | copy-start | bytes 4718596
  216.8 1.8 copy-start.19
  216.8 1.8 copy-start.34
  216.8 1.8 copy-start.44
  216.8 1.8 copy-start.49
  218.5 2.9 copy-start.7
  218.5 1.1 copy-start.24
  218.5 1.1 copy-start.45
  218.5 1.9 copy-start.50
  221.4 1.2 copy-start.11
  221.4 1.2 copy-start.32
  221.4 1.2 copy-start.15
  222.6 1.2 copy-start.10
  222.6 1.2 copy-start.40
  224.8 254.9 %reduce-scatter.3.cloned.1.call-start = ((), (), s32[]{:S(2)}) async-start(), calls=%async_computation.4 | async-start | bytes 11354112 | tf_op jit(solution)/shard_map/reduce_scatter | solution.py:482
  258.7 2.2 copy-start.6
  258.8 2.2 copy-start.55
  274.0 2.4 copy-start.12
  274.0 2.4 copy-start.33
  274.0 3.1 copy-start.5
  277.2 15.5 %copy-start.8 = (bf16[512,768]{1,0:T(8,128)(2,1)S(1)}, bf16[512,768]{1,0:T(8,128)(2,1)}, u32[]{:S(2)}) copy-start(bf16[512,768]{1,0:T(8,128)(2,1)} %copy-done.7) | copy-start | bytes 2359300
  279.6 8.5 %copy-start.47 = (bf16[3,192]{1,0:T(4,128)(2,1)S(1)}, bf16[3,192]{1,0:T(4,128)(2,1)}, u32[]{:S(2)}) copy-start(bf16[3,192]{1,0:T(4,128)(2,1)} %reduce.38) | copy-start | bytes 3460
  293.8 2.2 copy-start.16
  293.8 3.4 copy-start.35
  298.8 5.1 %copy-start.25 = (bf16[192,512]{1,0:T(8,128)(2,1)S(1)}, bf16[192,512]{1,0:T(8,128)(2,1)}, u32[]{:S(2)}) copy-start(bf16[192,512]{1,0:T(8,128)(2,1)} %get-tuple-element.30) | copy-start | bytes 589828
  300.4 3.8 copy-start.13
  300.4 3.8 copy-start.26
  303.9 1.2 copy-start.37
  304.6 0.7 copy-start.54
  304.6 0.7 copy-start.53
  304.6 0.8 copy-start.46
  304.7 0.8 copy-start.42
  304.7 0.8 copy-start.43
  304.7 0.8 copy-start.48
  304.7 1.0 copy-start.20
  304.7 1.0 copy-start.31
  306.8 1.9 copy-start.58
  307.0 2.0 copy-start.23
  307.8 4.0 slice-start
  309.0 2.9 slice-start.1
  317.0 2.6 copy-start.2
  317.0 3.0 copy-start.4
  479.7 3.8 copy-start.18
  (2 other events, 1.3 us)
Sparse Core Ops, SparseCore 0:
  13.2 90.9 all-gather.2
  107.1 62.2 all-gather.4
  224.9 105.9 reduce-scatter.4
  336.7 142.8 reduce-scatter.2

commit v2 on v1

--- a/solution.py
+++ b/solution.py
@@ -469,15 +469,18 @@
 
 
 def scatter_late(count, grad_attn, grad_first, small_grads):
-    width = grad_attn.shape[1]
-    rows = grad_attn.shape[0] // count
+    width = grad_first.shape[1]
+    rows = grad_first.shape[0] // count
     blocks = small_blocks(count, *small_grads)
     joined = jnp.concatenate(blocks, 1)
     size = joined.shape[1]
     small_rows = rows_for(size, width, rows % 8 == 0)
     joined = jnp.pad(joined, ((0, 0), (0, small_rows * width - size))).reshape(count, small_rows, width)
+    attn_rows = jnp.concatenate(
+        [part.astype(jnp.bfloat16).reshape(count, rows, -1) for part in grad_attn], 2
+    )
     packed = jnp.concatenate(
-        [grad_attn.reshape(count, rows, width), grad_first.reshape(count, rows, width), joined], 1
+        [attn_rows, grad_first.astype(jnp.bfloat16).reshape(count, rows, width), joined.astype(jnp.bfloat16)], 1
     )
     summed = lax.psum_scatter(
         packed.reshape(-1, width).astype(jnp.bfloat16), AXES, scatter_dimension=0, tiled=True
@@ -551,7 +554,7 @@
     out_part = jnp.einsum(
         "pds,pse->de", kept_all[2], text_first_low, preferred_element_type=jnp.float32
     )
-    summed = scatter_late(count, jnp.concatenate([three_part, out_part], 1), first_grad, totals)
+    summed = scatter_late(count, (three_part, out_part), first_grad, totals)
     return (
         out_text,
         out_layout,

time: 497 us -> 483 us (0.972)
  local copies, waits for them, and re-layouts: 86 us -> 68.3 us
  matrix products: 71.9 us -> 83.6 us
  other arithmetic: 35.3 us -> 29.7 us
    dot_general x1, matrix products: 4.45 us -> 15.6 us  [body(): jnp.einsum('sf,sd->fd', flat_rows(text_active), flat_rows(round_second),...]
    concatenate x1 -> x0, local copies, waits for them, and re-layouts: 6.62 us -> none  [body(): jnp.concatenate([three_part, out_part], 1)]
    unnamed x136 -> x150, local copies, waits for them, and re-layouts: 12.6 us -> 12.7 us
  transfers between devices with their start and end apart: 4 -> 4, of which waited for: 4 -> 4; matrix products, arithmetic and copies ran while one was open for 25% -> 26% of each run, Pallas kernels for 8% -> 8%
where the time goes in v2:
time: 483 us; the launch traced here: 478 us
  waiting for transfers between devices  243 us (50%)
  matrix products  83.6 us (17%)
  local copies, waits for them, and re-layouts  68.3 us (14%)
  Pallas kernels  37.3 us (8%)
  other arithmetic  29.7 us (6%)
  between operations  15.6 us (3%)
    reduce_scatter x1, waiting for transfers between devices, scatter_late(): lax.psum_scatter(packed.reshape(-1, width).astype(jnp.bfloat16), AXES, sc...  147 us
    all_gather x1, waiting for transfers between devices, gather_weights(): first_all = lax.all_gather(first, AXES, axis=0, tiled=True)  89 us
    pallas_call x1, Pallas kernels, attn_back_heads(): pl.pallas_call(functools.partial(attn_back_kernel, scales=scales), grid_s...  23.9 us
    dot_general x1, matrix products, body(): jnp.einsum('sf,sd->fd', flat_rows(text_active), flat_rows(round_second),...  15.6 us
    pallas_call x1, Pallas kernels, attn_fwd_heads(): pl.pallas_call(functools.partial(attn_fwd_kernel, scales=scales), grid_sp...  13.4 us
    unnamed x150, local copies, waits for them, and re-layouts  12.7 us
    dot_general x2, matrix products, branch_forward(): jnp.dot(hidden.astype(jnp.bfloat16), first, preferred_element_type=jnp.fl...  9.77 us
  transfers between devices with their start and end apart: 4, of which 4 were waited for; matrix products, arithmetic and copies ran while one was open for 26% of the time, Pallas kernels for 8%

profile of v2, /device:TPU:0, one launch (start us, length us, event | category | flops | bytes accessed | tf_op | source)
XLA Modules:
  0.0 478.1 jit_solution(18077976582474841656)
XLA Ops:
  9.8 1.5 concatenate.28
  11.3 1.7 pad_maximum_fusion.2
  15.1 89.0 %all-gather.3.cloned.1.call-done = bf16[1792,3072]{1,0:T(8,128)(2,1)} async-done(((bf16[56,3072]{1,0:T(8,128)(2,1)}), bf16[1792,3072]{1,0:T(8,128)(2,1)}) %all-gather.3.cloned.1.call-update) | async-done | bytes 11010064 | tf_op jit(solution)/shard_map/all_gather | solution.py:446
  104.2 1.5 slice.193
  105.7 0.9 copy.49
  110.8 1.0 reshape.623
  112.0 1.1 reshape.633
  113.1 2.5 reshape.631
  115.6 1.8 copy.35
  117.4 6.8 %fusion.69 = (bf16[32,24,3072]{2,1,0:T(8,128)(2,1)S(1)}, bf16[32,24,3072]{2,1,0:T(8,128)(2,1)}) fusion(bf16[32,56,3072]{2,1,0:T(8,128)(2,1)} %bitcast.229), kind=kLoop, calls=%fused_computation.158 | loop fusion | bytes 18874368 | tf_op jit(solution)/shard_map/slice | solution.py:449
  124.2 2.2 copy-done
  126.4 2.1 slice.192
  128.6 4.6 copy.33
  133.2 1.8 fusion.75
  136.5 2.2 fusion.14.layout_ref
  138.7 4.7 add_convert_fusion.text_ref
  143.4 13.4 %vmap__.2 = (bf16[768,512]{1,0:T(8,128)(2,1)}, bf16[192,512]{1,0:T(8,128)(2,1)}, f32[12,1,512]{2,1,0:T(1,128)}) custom-call(s32[1]{0:T(128)} %copy.62.len_ref, bf16[3,768,512]{2,1,0:T(8,128)(2,1)} %add_convert_fusion.text_ref, bf16[3,192,512]{2,1,0:T(8,128)(2,1)} %fusion.14.layout_ref), custom_call_target="tpu_custom_call" | custom-call | flops 1006632960 | bytes 3956736 | tf_op jit(solution)/shard_map/vmap()/pallas_call | solution.py:148
  156.8 2.7 fusion.76
  160.5 0.9 copy-done.21
  161.4 8.1 %add_bitcast_fusion = (f32[1,512,3072]{2,1,0:T(8,128)}, bf16[512,3072]{1,0:T(8,128)(2,1)}) fusion(f32[3072]{0:T(1024)S(1)} %slice-done, bf16[768,3072]{1,0:T(8,128)(2,1)} %bitcast.235, bf16[1,512,768]{2,1,0:T(8,128)(2,1)S(1)} %fusion.20), kind=kOutput, calls=%fused_computation.9 | convolution fusion | flops 2425356288 | bytes 14954496 | tf_op jit(solution)/shard_map/vmap()/dot_general | solution.py:212
  169.6 6.0 %fusion.77 = (f32[512]{0:T(512)S(1)}, f32[1,512,768]{2,1,0:T(8,128)S(1)}) fusion(f32[768]{0:T(1024)S(1)} %copy-done.50, bf16[512,3072]{1,0:T(8,128)(2,1)} %get-tuple-element.83, bf16[3072,768]{1,0:T(8,128)(2,1)} %all-gather.5.cloned.1.call-done, f32[768]{0:T(1024)S(1)} %copy-done.37, f32[768]{0:T(1024)S(1)} %get-tuple-element.98, ...), kind=kOutput, calls=%fused_computation.166 | convolution fusion | flops 2418671104 | bytes 11025408 | tf_op jit(solution)/shard_map/vmap()/dot_general | solution.py:216
  178.8 1.7 fusion.68
  180.8 0.9 copy-done.18
  181.6 1.1 copy-done.67
  182.7 15.6 %convolution_convert_fusion.2 = bf16[3072,768]{1,0:T(8,128)(2,1)} fusion(bf16[512,3072]{1,0:T(8,128)(2,1)S(1)} %copy-done.67, bf16[1,512,768]{2,1,0:T(8,128)(2,1)S(1)} %get-tuple-element.35), kind=kOutput, calls=%fused_computation.12 | convolution fusion | flops 2418278400 | bytes 8650752 | tf_op jit(solution)/shard_map/sf,sd->fd/dot_general | solution.py:535
  198.3 1.3 fusion.78
  199.8 1.7 multiply_convert_fusion.1
  203.4 0.9 fusion.65
  205.1 1.1 multiply_add_fusion
  206.2 1.2 multiply_reduce_fusion.8
  207.4 1.6 fusion.70
  209.2 0.9 fusion.25
  213.4 8.3 %fusion.80 = (bf16[3072]{0:T(1024)(128)(2,1)}, bf16[1,512,3072]{2,1,0:T(8,128)(2,1)S(1)}) fusion(f32[1,512,3072]{2,1,0:T(8,128)} %get-tuple-element.34, bf16[3072,768]{1,0:T(8,128)(2,1)} %all-gather.5.cloned.1.call-done, bf16[1,512,768]{2,1,0:T(8,128)(2,1)S(1)} %copy-done.19), kind=kOutput, calls=%fused_computation.169 | convolution fusion | flops 2437936128 | bytes 14948352 | tf_op jit(solution)/shard_map/vmap()/dot_general | solution.py:279
  221.7 8.2 %multiply_reduce_fusion = (bf16[768]{0:T(1024)(128)(2,1)}, f32[512]{0:T(512)S(1)}, bf16[768]{0:T(1024)(128)(2,1)}, f32[1,512,768]{2,1,0:T(8,128)}) fusion(f32[1,512,768]{2,1,0:T(8,128)S(1)} %get-tuple-element.36, f32[512]{0:T(512)S(1)} %fusion.59, f32[512]{0:T(512)S(1)} %broadcast_multiply_fusion.2, f32[768]{0:T(1024)S(1)} %get-tuple-element.98, ...), kind=kOutput, calls=%fused_computation.23 | convolution fusion | flops 2419456000 | bytes 12595200 | tf_op jit(solution)/shard_map/vmap()/dot_general | solution.py:283
  231.7 1.6 copy.39
  233.3 1.2 reduce_sum.419
  234.6 1.2 reduce_sum.421
  235.7 1.2 reduce_sum.428
  237.0 1.3 reduce_sum.426
  238.2 1.3 reduce_sum.440
  239.5 2.1 fusion.66
  241.7 1.2 fusion.24.dcl_ref
  242.8 3.1 fusion.15.dc_ref
  245.9 23.9 %vmap__.3 = (bf16[3,768,512]{2,1,0:T(8,128)(2,1)}, bf16[3,192,512]{2,1,0:T(8,128)(2,1)}) custom-call(s32[1]{0:T(128)} %copy.62.len_ref, bf16[3,768,512]{2,1,0:T(8,128)(2,1)} %add_convert_fusion.text_ref, bf16[768,512]{1,0:T(8,128)(2,1)} %fusion.15.dc_ref, bf16[3,192,512]{2,1,0:T(8,128)(2,1)} %fusion.14.layout_ref, bf16[192,512]{1,0:T(8,128)(2,1)} %fusion.24.dcl_ref, ...), custom_call_target="tpu_custom_call" | custom-call | flops 2013265920 | bytes 3956736 | tf_op jit(solution)/shard_map/vmap()/pallas_call | solution.py:100
  269.9 1.3 reduce.38
  271.2 1.4 convolution_convert_fusion.6
  272.7 1.0 reshape.646
  274.7 2.2 reduce.37
  278.6 1.0 reshape.648
  280.0 1.9 fusion.18
  281.9 2.0 copy.42
  283.9 3.0 reshape.647
  286.8 1.7 concatenate.34
  288.7 0.9 copy.50
  289.9 0.9 convolution_convert_fusion.3
  291.7 2.1 convolution_convert_fusion.1
  293.9 2.9 convolution_convert_fusion
  296.8 5.9 %pad_maximum_fusion = bf16[32,56,3072]{2,1,0:T(8,128)(2,1)} fusion(bf16[32,8,3072]{2,1,0:T(8,128)(2,1)S(1)} %bitcast.234, bf16[32,24,3072]{2,1,0:T(8,128)(2,1)S(1)} %bitcast.237, bf16[32,24,768]{2,1,0:T(8,128)(2,1)S(1)} %bitcast.247, bf16[32,24,2304]{2,1,0:T(8,128)(2,1)S(1)} %bitcast.245), kind=kLoop, calls=%fused_computation | loop fusion | flops 44040192 | bytes 22020096 | tf_op jit(solution)/shard_map/concatenate | solution.py:482
  302.7 2.5 fusion.19
  305.7 4.9 %bitcast_add_fusion = f32[1,512,768]{2,1,0:T(8,128)} fusion(bf16[3,768,512]{2,1,0:T(8,128)(2,1)} %get-tuple-element.40, bf16[768,3,768]{0,2,1:T(8,128)(2,1)S(1)} %bitcast.227, f32[1,512,768]{2,1,0:T(8,128)S(1)} %copy-done.4, f32[512]{0:T(512)S(1)} %copy-done.35), kind=kOutput, calls=%fused_computation.19 | convolution fusion | flops 1812725760 | bytes 9046016 | tf_op jit(solution)/shard_map/vmap(jes,dje->sd)/dot_general | solution.py:192
  310.6 6.0 %reduce-scatter.5.cloned.1.call-done = bf16[96,768]{1,0:T(8,128)(2,1)} async-done(((bf16[3072,768]{1,0:T(8,128)(2,1)}), bf16[96,768]{1,0:T(8,128)(2,1)}) %reduce-scatter.5.cloned.1.call-update) | async-done | bytes 147472 | tf_op jit(solution)/shard_map/reduce_scatter | solution.py:539
  316.6 1.6 convert_element_type.193
  318.3 147.4 %reduce-scatter.3.cloned.1.call-done = bf16[56,3072]{1,0:T(8,128)(2,1)} async-done(((bf16[1792,3072]{1,0:T(8,128)(2,1)}), bf16[56,3072]{1,0:T(8,128)(2,1)}) %reduce-scatter.3.cloned.1.call-update) | async-done | bytes 344080 | tf_op jit(solution)/shard_map/reduce_scatter | solution.py:485
  465.6 1.1 convert_element_type.192
  (235 shorter events, 31.8 us)
Async XLA Ops:
  7.2 97.0 %all-gather.3.cloned.1.call-start = ((), (), s32[]{:S(2)}) async-start(), calls=%async_computation.2 | async-start | bytes 11354112 | tf_op jit(solution)/shard_map/all_gather | solution.py:446
  13.0 156.6 %all-gather.5.cloned.1.call-start = ((), (), s32[]{:S(2)}) async-start(), calls=%async_computation.3 | async-start | bytes 4866048 | tf_op jit(solution)/shard_map/all_gather | solution.py:454
  13.8 302.8 %reduce-scatter.5.cloned.1.call-start = ((), (), s32[]{:S(2)}) async-start(), calls=%async_computation.5 | async-start | bytes 4866048 | tf_op jit(solution)/shard_map/reduce_scatter | solution.py:539
  108.2 2.6 copy-start.26
  124.2 2.2 copy-start
  128.6 7.2 %copy-start.39 = (f32[1,768]{1,0:T(1,128)S(1)}, f32[1,768]{1,0:T(1,128)}, u32[]{:S(2)}) copy-start(f32[1,768]{1,0:T(1,128)} %stack.19) | copy-start | bytes 9220
  133.2 10.2 %copy-start.1 = (bf16[768,2304]{0,1:T(8,128)(2,1)}, bf16[768,2304]{0,1:T(8,128)(2,1)S(1)}, u32[]{:S(2)}) copy-start(bf16[768,2304]{0,1:T(8,128)(2,1)S(1)} %copy.33) | copy-start | bytes 10616836
  143.4 13.4 %copy-start.51 = (f32[768]{0:T(1024)S(1)}, f32[768]{0:T(1024)}, u32[]{:S(2)}) copy-start(f32[768]{0:T(1024)} %get-tuple-element.99) | copy-start | bytes 9220
  159.8 1.6 slice-start
  161.4 8.3 %copy-start.50 = (f32[768]{0:T(1024)S(1)}, f32[768]{0:T(1024)}, u32[]{:S(2)}) copy-start(f32[768]{0:T(1024)} %get-tuple-element.96) | copy-start | bytes 9220
  176.0 2.8 copy-start.38
  180.5 2.2 copy-start.67
  182.7 15.6 %copy-start.52 = (f32[192]{0:T(256)S(1)}, f32[192]{0:T(256)}, u32[]{:S(2)}) copy-start(f32[192]{0:T(256)} %get-tuple-element.107) | copy-start | bytes 2308
  199.7 1.8 copy-start.16
  199.7 1.8 copy-start.32
  199.7 1.8 copy-start.43
  199.7 1.8 copy-start.48
  201.5 2.9 copy-start.8
  201.5 1.1 copy-start.20
  201.5 1.9 copy-start.49
  204.4 1.8 copy-start.10
  204.4 1.8 copy-start.30
  205.1 1.1 copy-start.12
  207.4 1.8 copy-start.23
  210.8 254.8 %reduce-scatter.3.cloned.1.call-start = ((), (), s32[]{:S(2)}) async-start(), calls=%async_computation.4 | async-start | bytes 11354112 | tf_op jit(solution)/shard_map/reduce_scatter | solution.py:485
  212.3 1.1 copy-start.19
  213.0 8.7 %copy-start.36 = (f32[512]{0:T(512)}, f32[512]{0:T(512)S(1)}, u32[]{:S(2)}) copy-start(f32[512]{0:T(512)S(1)} %broadcast_multiply_fusion.2) | copy-start | bytes 6148
  213.4 8.3 %copy-start.46 = (f32[512]{0:T(512)}, f32[512]{0:T(512)S(1)}, u32[]{:S(2)}) copy-start(f32[512]{0:T(512)S(1)} %fusion.59) | copy-start | bytes 6148
  221.7 8.3 %copy-start.65 = (bf16[1,512,3072]{2,1,0:T(8,128)(2,1)}, bf16[1,512,3072]{2,1,0:T(8,128)(2,1)S(1)}, u32[]{:S(2)}) copy-start(bf16[1,512,3072]{2,1,0:T(8,128)(2,1)S(1)} %get-tuple-element.125) | copy-start | bytes 9437188
  221.7 8.8 %copy-start.62 = (bf16[192]{0:T(256)(128)(2,1)S(1)}, bf16[192]{0:T(256)(128)(2,1)}, u32[]{:S(2)}) copy-start(bf16[192]{0:T(256)(128)(2,1)} %get-tuple-element.66) | copy-start | bytes 1156
  221.7 9.4 %copy-start.61 = (bf16[192]{0:T(256)(128)(2,1)S(1)}, bf16[192]{0:T(256)(128)(2,1)}, u32[]{:S(2)}) copy-start(bf16[192]{0:T(256)(128)(2,1)} %get-tuple-element.69) | copy-start | bytes 1156
  239.5 2.1 copy-start.6
  239.5 2.1 copy-start.17
  241.6 48.0 %copy-start.3 = (f32[1,512,768]{2,1,0:T(8,128)}, f32[1,512,768]{2,1,0:T(8,128)S(1)}, u32[]{:S(2)}) copy-start(f32[1,512,768]{2,1,0:T(8,128)S(1)} %get-tuple-element.75) | copy-start | bytes 4718596
  241.6 35.3 %copy-start.34 = (f32[512]{0:T(512)}, f32[512]{0:T(512)S(1)}, u32[]{:S(2)}) copy-start(f32[512]{0:T(512)S(1)} %negate_multiply_fusion.2) | copy-start | bytes 6148
  245.9 25.3 %copy-start.24 = (bf16[1,512,192]{1,2,0:T(8,128)(2,1)S(1)}, bf16[1,512,192]{1,2,0:T(8,128)(2,1)}, u32[]{:S(2)}) copy-start(bf16[1,512,192]{1,2,0:T(8,128)(2,1)} %param.14) | copy-start | bytes 589828
  269.8 2.8 copy-start.25
  269.8 3.9 copy-start.40
  269.8 3.9 copy-start.55
  269.9 3.9 copy-start.56
  269.9 3.9 copy-start.57
  269.9 3.9 copy-start.58
  269.9 3.9 copy-start.59
  269.9 3.9 copy-start.60
  274.6 2.5 copy-start.54
  274.6 2.5 copy-start.53
  274.6 2.6 copy-start.45
  274.6 2.6 copy-start.41
  274.6 2.6 copy-start.42
  274.7 2.6 copy-start.47
  274.7 3.4 copy-start.9
  274.7 3.4 copy-start.11
  274.7 3.4 copy-start.31
  278.5 1.2 copy-start.13
  278.5 1.5 copy-start.33
  281.9 4.9 %copy-start.27 = (bf16[32,288]{1,0:T(8,128)(2,1)S(1)}, bf16[32,288]{1,0:T(8,128)(2,1)}, u32[]{:S(2)}) copy-start(bf16[32,288]{1,0:T(8,128)(2,1)} %reshape.643) | copy-start | bytes 55300
  281.9 4.9 %copy-start.29 = (bf16[32,72]{1,0:T(8,128)(2,1)S(1)}, bf16[32,72]{1,0:T(8,128)(2,1)}, u32[]{:S(2)}) copy-start(bf16[32,72]{1,0:T(8,128)(2,1)} %reshape.649) | copy-start | bytes 13828
  289.9 1.7 copy-start.7
  289.9 1.9 copy-start.63
  291.7 2.1 copy-start.22
  291.7 2.2 copy-start.66
  302.7 2.6 copy-start.2
  302.7 3.0 copy-start.4
  465.6 2.4 copy-start.15
  (9 other events, 8.3 us)
Sparse Core Ops, SparseCore 0:
  13.2 90.9 all-gather.2
  107.1 62.5 all-gather.4
  210.9 105.6 reduce-scatter.4
  322.5 143.1 reduce-scatter.2
